TPU v7x, 32 devices: a whole 2x2x4 slice. The times are simulated.
32 devices in a mesh: ctx: 16 (over z, x, core), head: 2 (over y).
Axes of the slice: x: 2, y: 2, z: 4, core: 2. Of those that a mesh axis runs over, the one named last changes fastest.
Arguments:
- queries: bfloat16 [8192, 1024], P('ctx', 'head'), may hold values from -6 to 6
- key_rows: bfloat16 [8192, 1024], P('ctx', 'head'), may hold values from -6 to 6
- values: bfloat16 [8192, 1024], P('ctx', 'head'), may hold values from -6 to 6
- outputs: bfloat16 [8192, 1024], P('ctx', 'head'), may hold values from -6 to 6
- out_grad: bfloat16 [8192, 1024], P('ctx', 'head'), may hold values from -48 to 48
- log_norm: bfloat16 [8, 8192], P('head', 'ctx'), may hold values from 4.5 to 7.5
- rand_blocks: int32 [64, 3], P('ctx'), may hold values from -1 to 61, as said below
Outputs:
- query_grad: bfloat16 [8192, 1024], P('ctx', 'head')
- key_grad: bfloat16 [8192, 1024], P('ctx', 'head')
- value_grad: bfloat16 [8192, 1024], P('ctx', 'head')
Inputs may be any that keep to these rules, and one draw needn't show every extreme that they name: `rand_blocks`: an entry of row j is a sequence block index of a key block for the query block of row j, or -1 for none. A named block lies between 1 and that query block's sequence index minus 2; the blocks named in the 4 rows of one index of ctx lie on distinct indices of ctx, none of them index 0.
All inputs are finite; a program needn't handle non-finite values.
Results may differ from a plain program's by a relative error of at most 0.0065.
Values may be sent and summed in bfloat16 or wider, within the bound.
No kernel may reach another device: no remote copies, remote signals or barrier semaphores. Data moves between devices by JAX's collectives and lax.ppermute only.
A program may use at most 128 MiB of HBM per device.

v0:
```python
import jax
import jax.numpy as jnp
from jax import lax
from jax.sharding import PartitionSpec as P

PAIR = 2
WINDOW = 2
GLOBAL = 1
RANDOM = 3


def padded(cells, sides, width):
    for axis, dim in sides:
        count = lax.axis_size(axis)
        ends = count - 1
        head = lax.slice_in_dim(cells, 0, width, axis=dim)
        tail = lax.slice_in_dim(cells, cells.shape[dim] - width, cells.shape[dim], axis=dim)
        cells = jnp.concatenate(
            [
                lax.ppermute(tail, axis, [(i, (i + 1) % count) for i in range(ends)]),
                cells,
                lax.ppermute(head, axis, [((i + 1) % count, i) for i in range(ends)]),
            ],
            axis=dim,
        )
    return cells


def spread_2(array, axis, root):
    mine = lax.axis_index(axis) == root
    return lax.psum(jnp.where(mine, array, jnp.zeros_like(array)), axis)


def pair_grads(query_heads, grad_heads, norm_blk, delta_blk, key_heads, value_heads, visible):
    head_size = query_heads.shape[-1]
    scaling = head_size ** (-0.5)
    scores = (
        jnp.einsum("nhid,nhjd->nhij", query_heads, key_heads, preferred_element_type=jnp.float32)
        * scaling
    )
    attn_prob = jnp.exp(scores - norm_blk.astype(jnp.float32)[:, :, :, None]) * visible[:, None]
    prob_low = attn_prob.astype(jnp.bfloat16)
    value_term = jnp.einsum(
        "nhij,nhid->nhjd", prob_low, grad_heads, preferred_element_type=jnp.float32
    )
    grad_prob = jnp.einsum(
        "nhid,nhjd->nhij", grad_heads, value_heads, preferred_element_type=jnp.float32
    )
    score_low = (attn_prob * (grad_prob - delta_blk.astype(jnp.float32)[:, :, :, None])).astype(
        jnp.bfloat16
    )
    query_term = (
        jnp.einsum("nhij,nhjd->nhid", score_low, key_heads, preferred_element_type=jnp.float32)
        * scaling
    )
    key_term = (
        jnp.einsum("nhij,nhid->nhjd", score_low, query_heads, preferred_element_type=jnp.float32)
        * scaling
    )
    return (query_term, key_term, value_term)


def shards(queries, key_rows, values, outputs, out_grad, log_norm, rand_blocks):
    ctx_size = lax.axis_size("ctx")
    my_index = lax.axis_index("ctx")
    row_count, features = queries.shape
    head_count = log_norm.shape[0]
    head_size = features // head_count
    slot_count = 2 * PAIR
    height = row_count // slot_count
    block_total = slot_count * ctx_size
    block_shape = (slot_count, head_count, height, head_size)

    def heads_major(array):
        return jnp.transpose(array.reshape(slot_count, height, head_count, head_size), (0, 2, 1, 3))

    query_blk = heads_major(queries)
    key_blk = heads_major(key_rows)
    value_blk = heads_major(values)
    output_blk = heads_major(outputs)
    grad_blk = heads_major(out_grad)
    norm_blk = jnp.transpose(log_norm.reshape(head_count, slot_count, height), (1, 0, 2))
    delta_blk = jnp.sum(
        grad_blk.astype(jnp.float32) * output_blk.astype(jnp.float32), axis=-1
    ).astype(jnp.bfloat16)
    within = jnp.arange(slot_count, dtype=jnp.int32)
    seq_blk = jnp.where(
        within < PAIR, PAIR * my_index + within, block_total - 1 - PAIR * my_index - (within - PAIR)
    )
    last_dev = my_index == ctx_size - 1
    first_dev = my_index == 0
    causal = jnp.tril(jnp.ones((height, height), jnp.float32))
    self_query, self_key, self_value = pair_grads(
        query_blk,
        grad_blk,
        norm_blk,
        delta_blk,
        key_blk,
        value_blk,
        jnp.broadcast_to(causal, (slot_count, height, height)),
    )
    rim_keys = jnp.stack(
        [
            jnp.stack([key_blk[PAIR], key_blk[PAIR - 1]]),
            jnp.stack([value_blk[PAIR], value_blk[PAIR - 1]]),
        ]
    )
    widened = padded(rim_keys, (("ctx", 1),), 1)
    tail_key = jnp.where(last_dev, key_blk[PAIR - 1], widened[0, 3])
    tail_value = jnp.where(last_dev, value_blk[PAIR - 1], widened[1, 3])
    prev_keys = jnp.concatenate(
        [widened[0, 0][None], key_blk[0 : PAIR - 1], key_blk[PAIR + 1 : slot_count], tail_key[None]]
    )
    prev_values = jnp.concatenate(
        [
            widened[1, 0][None],
            value_blk[0 : PAIR - 1],
            value_blk[PAIR + 1 : slot_count],
            tail_value[None],
        ]
    )
    visible = jnp.where((within == 0) & first_dev, 0.0, 1.0).astype(jnp.float32)[:, None, None]
    window_query, term_key, term_value = pair_grads(
        query_blk, grad_blk, norm_blk, delta_blk, prev_keys, prev_values, visible
    )
    out_rim = jnp.stack(
        [
            jnp.stack([term_key[0], term_key[slot_count - 1]]),
            jnp.stack([term_value[0], term_value[slot_count - 1]]),
        ]
    )
    came_back = padded(out_rim.astype(jnp.bfloat16), (("ctx", 1),), 1).astype(out_rim.dtype)
    own_tail = jnp.where(last_dev, 1.0, 0.0).astype(jnp.float32)

    def spread(term, returned):
        return jnp.concatenate(
            [
                term[1:PAIR],
                (term[slot_count - 1] * own_tail + returned[3])[None],
                returned[0][None],
                term[PAIR : slot_count - 1],
            ]
        )

    window_key = spread(term_key, came_back[0])
    window_value = spread(term_value, came_back[1])
    global_kv = spread_2(jnp.stack([key_blk[0:GLOBAL], value_blk[0:GLOBAL]]), "ctx", 0)
    target = jnp.repeat(jnp.arange(GLOBAL, dtype=jnp.int32), slot_count)
    visible_glob = (jnp.tile(seq_blk, GLOBAL) >= target + WINDOW).astype(jnp.float32)[:, None, None]
    glob_query, glob_key, glob_value = pair_grads(
        jnp.tile(query_blk, (GLOBAL, 1, 1, 1)),
        jnp.tile(grad_blk, (GLOBAL, 1, 1, 1)),
        jnp.tile(norm_blk, (GLOBAL, 1, 1)),
        jnp.tile(delta_blk, (GLOBAL, 1, 1)),
        jnp.repeat(global_kv[0], slot_count, axis=0),
        jnp.repeat(global_kv[1], slot_count, axis=0),
        visible_glob,
    )
    glob_query = jnp.sum(glob_query.reshape((GLOBAL,) + block_shape), axis=0)
    part_key = jnp.sum(glob_key.reshape((GLOBAL,) + block_shape), axis=1)
    part_value = jnp.sum(glob_value.reshape((GLOBAL,) + block_shape), axis=1)
    total_key, total_value = lax.psum((part_key, part_value), "ctx")
    owner_flag = jnp.where(first_dev, 1.0, 0.0).astype(jnp.float32)
    padding = jnp.zeros((slot_count - GLOBAL,) + block_shape[1:], jnp.float32)
    glob_key_add = jnp.concatenate([total_key * owner_flag, padding])
    glob_value_add = jnp.concatenate([total_value * owner_flag, padding])
    ref_valid = rand_blocks >= 0
    in_front = rand_blocks < block_total // 2
    mirror = block_total - 1 - rand_blocks
    owner_dev = jnp.where(in_front, rand_blocks // PAIR, mirror // PAIR)
    owner_dev = jnp.where(ref_valid, owner_dev, ctx_size).reshape(-1)
    key_slot = jnp.where(in_front, rand_blocks % PAIR, PAIR + mirror % PAIR) + 1
    key_slot = jnp.where(ref_valid, key_slot, 0).reshape(-1)
    targets = jnp.arange(ctx_size, dtype=jnp.int32)
    matches = owner_dev[None, :] == targets[:, None]
    slot_send = jnp.sum(jnp.where(matches, key_slot[None, :], 0), axis=1)
    key_flat = key_blk.reshape(slot_count, -1)
    value_flat = value_blk.reshape(slot_count, -1)
    slot_ids = jnp.arange(1, slot_count + 1, dtype=jnp.int32)
    select = jnp.any(matches.reshape(ctx_size, slot_count, RANDOM), axis=2).astype(jnp.bfloat16)

    def route_rows(block):
        return jnp.dot(
            select, block.reshape(slot_count, -1), preferred_element_type=jnp.float32
        ).astype(jnp.bfloat16)

    arrived = (
        lax.all_to_all(route_rows(query_blk), "ctx", split_axis=0, concat_axis=0, tiled=True),
        lax.all_to_all(route_rows(grad_blk), "ctx", split_axis=0, concat_axis=0, tiled=True),
        lax.all_to_all(route_rows(norm_blk), "ctx", split_axis=0, concat_axis=0, tiled=True),
        lax.all_to_all(route_rows(delta_blk), "ctx", split_axis=0, concat_axis=0, tiled=True),
        lax.all_to_all(slot_send, "ctx", split_axis=0, concat_axis=0, tiled=True),
    )
    group_size = 8
    rounds = ctx_size // group_size
    item_shape = (group_size,) + block_shape[1:]
    stat_shape = (group_size, head_count, height)

    def owner_step(carry, item):
        query_item, grad_item, norm_item, delta_item, slot_item = item
        choose = slot_item[:, None] == slot_ids[None, :]
        choose_low = choose.astype(jnp.bfloat16)
        key_item = (
            jnp.dot(choose_low, key_flat, preferred_element_type=jnp.float32)
            .astype(jnp.bfloat16)
            .reshape(item_shape)
        )
        value_item = (
            jnp.dot(choose_low, value_flat, preferred_element_type=jnp.float32)
            .astype(jnp.bfloat16)
            .reshape(item_shape)
        )
        visible_rand = (slot_item > 0).astype(jnp.float32)[:, None, None]
        term_query, term_key, term_value = pair_grads(
            query_item.reshape(item_shape),
            grad_item.reshape(item_shape),
            norm_item.reshape(stat_shape),
            delta_item.reshape(stat_shape),
            key_item,
            value_item,
            visible_rand,
        )
        choose_float = choose.astype(jnp.float32)
        key_acc = carry[0] + jnp.einsum(
            "gs,gx->sx",
            choose_float,
            term_key.reshape(group_size, -1),
            precision=lax.Precision.HIGHEST,
        )
        value_acc = carry[1] + jnp.einsum(
            "gs,gx->sx",
            choose_float,
            term_value.reshape(group_size, -1),
            precision=lax.Precision.HIGHEST,
        )
        return ((key_acc, value_acc), term_query.astype(jnp.bfloat16).reshape(group_size, -1))

    def regroup(array):
        return array.reshape((rounds, group_size) + array.shape[1:])

    zero_acc = jnp.zeros((slot_count, height * features), jnp.float32)
    (rand_key, rand_value), answers = lax.scan(
        owner_step,
        (zero_acc, zero_acc),
        (
            regroup(arrived[0]),
            regroup(arrived[1]),
            regroup(arrived[2]),
            regroup(arrived[3]),
            regroup(arrived[4]),
        ),
    )
    answers = answers.reshape(ctx_size, height * features)
    returned = lax.all_to_all(answers, "ctx", split_axis=0, concat_axis=0, tiled=True)
    rand_query = jnp.dot(select.T, returned, preferred_element_type=jnp.float32)
    query_total = self_query + window_query + glob_query + rand_query.reshape(block_shape)
    key_total = self_key + window_key + glob_key_add + rand_key.reshape(block_shape)
    value_total = self_value + window_value + glob_value_add + rand_value.reshape(block_shape)

    def rows_major(array):
        return jnp.transpose(array.astype(jnp.bfloat16), (0, 2, 1, 3)).reshape(row_count, features)

    return (rows_major(query_total), rows_major(key_total), rows_major(value_total))


def solution(mesh):
    return jax.shard_map(
        shards,
        mesh=mesh,
        in_specs=(
            P("ctx", "head"),
            P("ctx", "head"),
            P("ctx", "head"),
            P("ctx", "head"),
            P("ctx", "head"),
            P("head", "ctx"),
            P("ctx", None),
        ),
        out_specs=(P("ctx", "head"), P("ctx", "head"), P("ctx", "head")),
        check_vma=False,
    )
```

profile of v0, /device:TPU:1, one launch (start us, length us, event | category | flops | bytes accessed | tf_op | source)
XLA Modules:
  0.0 470.3 jit_solution(4784505163282766554)
XLA Ops:
  8.8 7.3 %all-to-all-start = ((s32[16,1,1]{2,1,0:T(1,128)}), s32[16,1,1]{2,1,0:T(1,128)S(1)}, u32[]{:S(2)}, u32[]{:S(2)}) async-start(s32[16,1,1]{2,1,0:T(1,128)} %copy.127), calls=%async_computation | async-start | bytes 16384 | tf_op jit(solution)/shard_map/all_to_all | solution.py:192
  21.9 5.6 %all-to-all-start.4 = ((bf16[16,2,256]{2,1,0:T(2,128)(2,1)}), bf16[16,2,256]{2,1,0:T(2,128)(2,1)S(1)}, u32[]{:S(2)}, u32[]{:S(2)}) async-start(bf16[16,2,256]{2,1,0:T(2,128)(2,1)} %reshape.287), calls=%async_computation.4 | async-start | bytes 32768 | tf_op jit(solution)/shard_map/all_to_all | solution.py:191
  29.0 4.3 all-to-all-done.4
  33.3 4.0 all-to-all-start.2
  38.1 2.9 reduce.7
  41.0 4.0 reshape.285
  45.0 6.1 %all-to-all-start.3 = ((bf16[16,2,32768]{2,1,0:T(2,128)(2,1)}), bf16[16,2,32768]{2,1,0:T(2,128)(2,1)S(1)}, u32[]{:S(2)}, u32[]{:S(2)}) async-start(bf16[16,2,32768]{2,1,0:T(2,128)(2,1)} %reshape.285), calls=%async_computation.3 | async-start | bytes 4194304 | tf_op jit(solution)/shard_map/all_to_all | solution.py:189
  53.3 2.0 reshape.243
  58.3 2.0 collective-permute-start.1
  60.3 3.6 collective-permute-start
  63.8 2.0 reshape.239
  66.9 2.2 fusion.24
  69.1 4.5 reduce.5
  73.6 4.0 reshape.281
  77.6 15.0 %all-to-all-done.3 = bf16[16,2,32768]{2,1,0:T(2,128)(2,1)S(1)} async-done(((bf16[16,2,32768]{2,1,0:T(2,128)(2,1)}), bf16[16,2,32768]{2,1,0:T(2,128)(2,1)S(1)}, u32[]{:S(2)}, u32[]{:S(2)}) %all-to-all-start.3) | async-done | bytes 2097184 | tf_op jit(solution)/shard_map/all_to_all | solution.py:189
  92.7 12.4 %all-to-all-start.1 = ((bf16[16,2,32768]{2,1,0:T(2,128)(2,1)}), bf16[16,2,32768]{2,1,0:T(2,128)(2,1)}, u32[]{:S(2)}, u32[]{:S(2)}) async-start(bf16[16,2,32768]{2,1,0:T(2,128)(2,1)} %reshape.281), calls=%async_computation.1 | async-start | bytes 4194304 | tf_op jit(solution)/shard_map/all_to_all | solution.py:188
  105.0 2.9 copy_bitcast_fusion.6
  109.2 1.8 fusion.46
  115.7 1.8 slice_bitcast_fusion.7
  124.6 6.8 %reshape.286 = bf16[16,1,65536]{2,1,0:T(2,128)(2,1)} reshape(bf16[16,2,32768]{2,1,0:T(2,128)(2,1)S(1)} %all-to-all-done.3) | data formatting | bytes 4194304
  131.4 4.5 copy.278
  135.8 10.6 %all-to-all-done.1 = bf16[16,2,32768]{2,1,0:T(2,128)(2,1)} async-done(((bf16[16,2,32768]{2,1,0:T(2,128)(2,1)}), bf16[16,2,32768]{2,1,0:T(2,128)(2,1)}, u32[]{:S(2)}, u32[]{:S(2)}) %all-to-all-start.1) | async-done | bytes 2097184 | tf_op jit(solution)/shard_map/all_to_all | solution.py:188
  146.4 10.4 %reshape.282 = bf16[16,1,65536]{2,1,0:T(2,128)(2,1)} reshape(bf16[16,2,32768]{2,1,0:T(2,128)(2,1)} %all-to-all-done.1) | data formatting | bytes 4194304
  156.9 5.9 %copy.279 = bf16[16,1,65536]{2,0,1:T(8,128)(2,1)} copy(bf16[16,1,65536]{2,1,0:T(2,128)(2,1)} %reshape.282) | data formatting | bytes 4194304
  162.7 48.4 %while.15 = (s32[]{:T(128)}, f32[4,65536]{1,0:T(4,128)}, f32[4,65536]{1,0:T(4,128)}, bf16[2,8,65536]{2,1,0:T(8,128)(2,1)}, s32[2,8]{1,0:T(2,128)S(1)}, /*index=5...) while((s32[]{:T(128)}, f32[4,65536]{1,0:T(4,128)}, ...), condition=%wide.region_5.6_spmd.clone, body=%wide.region_4.5_spmd.clone.sunk | while | flops 737157248 | bytes 105006344 | solution.py:242
  162.9 1.9 convolution_convert_fusion.8
  167.8 1.9 convolution_convert_fusion.9
  172.8 2.4 constant_dynamic-update-slice_fusion.2
  175.2 1.8 convolution_multiply_fusion.8
  177.0 4.4 convolution_add_fusion.7
  183.1 2.9 convolution_add_fusion.8
  187.0 1.9 convolution_convert_fusion.8
  191.9 1.9 convolution_convert_fusion.9
  196.9 2.4 constant_dynamic-update-slice_fusion.2
  199.4 1.8 convolution_multiply_fusion.8
  201.2 4.4 convolution_add_fusion.7
  207.3 2.9 convolution_add_fusion.8
  211.2 3.8 reduce.9
  215.0 2.8 reshape.289
  217.8 11.0 %all-to-all-start.5 = ((bf16[16,2,32768]{2,1,0:T(2,128)(2,1)}), bf16[16,2,32768]{2,1,0:T(2,128)(2,1)}, u32[]{:S(2)}, u32[]{:S(2)}) async-start(bf16[16,2,32768]{2,1,0:T(2,128)(2,1)} %reshape.289), calls=%async_computation.5 | async-start | bytes 4194304 | tf_op jit(solution)/shard_map/all_to_all | solution.py:254
  230.2 3.7 collective-permute-start.2
  233.9 1.9 collective-permute-start.3
  238.4 104.7 %all-reduce.6.cloned.1.call-done = bf16[2,1,4,128,128]{4,3,2,1,0:T(8,128)(2,1)} async-done(((bf16[2,1,4,128,128]{4,3,2,1,0:T(8,128)(2,1)}), bf16[2,1,4,128,128]{4,3,2,1,0:T(8,128)(2,1)}) %all-reduce.6.cloned.1.call-update) | async-done | bytes 262160 | tf_op jit(solution)/shard_map/psum | solution.py:31
  347.9 1.8 convert_bitcast_fusion.3
  349.7 2.7 fusion.135
  352.4 86.0 %all-reduce.8.cloned.1.call-done = (f32[1,4,128,128]{3,2,1,0:T(8,128)}, f32[1,4,128,128]{3,2,1,0:T(8,128)}) async-done(((f32[1,4,128,128]{3,2,1,0:T(8,128)}, f32[1,4,128,128]{3,2,1,0:T(8,128)}), (f32[1,4,128,128]{3,2,1,0:T(8,128)}, f32[1,4,128,128]{3,2,1,0:T(8,128)})) %all-reduce.8.cloned.1.call-update) | async-done | bytes 524304 | tf_op jit(solution)/shard_map/psum | solution.py:162
  444.6 10.4 %reshape.290 = bf16[16,1,65536]{2,1,0:T(2,128)(2,1)} reshape(bf16[16,2,32768]{2,1,0:T(2,128)(2,1)} %all-to-all-done.5) | data formatting | bytes 4194304
  455.1 4.5 copy.277
  (251 shorter events, 64.0 us)
Async XLA Ops:
  8.8 13.0 %all-to-all-start = ((s32[16,1,1]{2,1,0:T(1,128)}), s32[16,1,1]{2,1,0:T(1,128)S(1)}, u32[]{:S(2)}, u32[]{:S(2)}) async-start(s32[16,1,1]{2,1,0:T(1,128)} %copy.127), calls=%async_computation | async-start | bytes 16384 | tf_op jit(solution)/shard_map/all_to_all | solution.py:192
  16.3 11.2 %copy-start.54 = (bf16[4,512]{1,0:T(4,128)(2,1)S(1)}, bf16[4,512]{1,0:T(4,128)(2,1)}, u32[]{:S(2)}) copy-start(bf16[4,512]{1,0:T(4,128)(2,1)} %param.14) | copy-start | bytes 12292
  17.4 104.1 %copy-start.10 = (bf16[4,128,4,128]{3,2,1,0:T(4,128)(2,1)}, bf16[4,128,4,128]{3,2,1,0:T(4,128)(2,1)S(1)}, u32[]{:S(2)}) copy-start(bf16[4,128,4,128]{3,2,1,0:T(4,128)(2,1)S(1)} %reshape.242) | copy-start | bytes 1572868
  19.1 47.8 %copy-start.52 = (pred[16,4]{0,1:T(4,128)(4,1)}, pred[16,4]{0,1:T(4,128)(4,1)S(1)}, u32[]{:S(2)}) copy-start(pred[16,4]{0,1:T(4,128)(4,1)S(1)} %fusion.98) | copy-start | bytes 196
  21.9 11.4 %all-to-all-start.4 = ((bf16[16,2,256]{2,1,0:T(2,128)(2,1)}), bf16[16,2,256]{2,1,0:T(2,128)(2,1)S(1)}, u32[]{:S(2)}, u32[]{:S(2)}) async-start(bf16[16,2,256]{2,1,0:T(2,128)(2,1)} %reshape.287), calls=%async_computation.4 | async-start | bytes 32768 | tf_op jit(solution)/shard_map/all_to_all | solution.py:191
  33.3 11.8 %all-to-all-start.2 = ((bf16[16,2,256]{2,1,0:T(2,128)(2,1)}), bf16[16,2,256]{2,1,0:T(2,128)(2,1)S(1)}, u32[]{:S(2)}, u32[]{:S(2)}) async-start(bf16[16,2,256]{2,1,0:T(2,128)(2,1)} %reshape.283), calls=%async_computation.2 | async-start | bytes 32768 | tf_op jit(solution)/shard_map/all_to_all | solution.py:190
  45.0 47.6 %all-to-all-start.3 = ((bf16[16,2,32768]{2,1,0:T(2,128)(2,1)}), bf16[16,2,32768]{2,1,0:T(2,128)(2,1)S(1)}, u32[]{:S(2)}, u32[]{:S(2)}) async-start(bf16[16,2,32768]{2,1,0:T(2,128)(2,1)} %reshape.285), calls=%async_computation.3 | async-start | bytes 4194304 | tf_op jit(solution)/shard_map/all_to_all | solution.py:189
  58.3 57.5 %collective-permute-start.1 = (bf16[2,1,4,128,128]{4,3,2,1,0:T(8,128)(2,1)S(1)}, bf16[2,1,4,128,128]{4,3,2,1,0:T(8,128)(2,1)}, u32[]{:S(2)}, u32[]{:S(2)}) collective-permute-start(bf16[2,1,4,128,128]{4,3,2,1,0:T(8,128)(2,1)S(1)} %get-tuple-element.165), channel_id=1, source_target_pairs={{2,0},{4,2},{6,4},{8,6},{10,8},{12,10},{14,12},{16,14},{18,16},{20... | collective-permute-start | bytes 786440 | tf_op jit(solution)/shard_map/ppermute | solution.py:22
  60.3 59.0 %collective-permute-start = (bf16[2,1,4,128,128]{4,3,2,1,0:T(8,128)(2,1)}, bf16[2,1,4,128,128]{4,3,2,1,0:T(8,128)(2,1)}, u32[]{:S(2)}, u32[]{:S(2)}) collective-permute-start(bf16[2,1,4,128,128]{4,3,2,1,0:T(8,128)(2,1)} %get-tuple-element.164), channel_id=1, source_target_pairs={{0,2},{2,4},{4,6},{6,8},{8,10},{10,12},{12,14},{14,16},{16,18},{18... | collective-permute-start | bytes 786440 | tf_op jit(solution)/shard_map/ppermute | solution.py:20
  92.7 53.8 %all-to-all-start.1 = ((bf16[16,2,32768]{2,1,0:T(2,128)(2,1)}), bf16[16,2,32768]{2,1,0:T(2,128)(2,1)}, u32[]{:S(2)}, u32[]{:S(2)}) async-start(bf16[16,2,32768]{2,1,0:T(2,128)(2,1)} %reshape.281), calls=%async_computation.1 | async-start | bytes 4194304 | tf_op jit(solution)/shard_map/all_to_all | solution.py:188
  107.9 3.6 copy-start.49
  107.9 3.0 copy-start.14
  109.2 3.6 copy-start.18
  115.1 5.2 %copy-start.15 = (bf16[4,128,4,128]{3,2,1,0:T(4,128)(2,1)S(1)}, bf16[4,128,4,128]{3,2,1,0:T(4,128)(2,1)}, u32[]{:S(2)}) copy-start(bf16[4,128,4,128]{3,2,1,0:T(4,128)(2,1)} %reshape.239) | copy-start | bytes 1572868
  115.1 5.2 %copy-start.56 = (f32[4,4,128]{2,1,0:T(4,128)S(1)}, f32[4,4,128]{2,1,0:T(4,128)}, u32[]{:S(2)}) copy-start(f32[4,4,128]{2,1,0:T(4,128)} %copy-done.55) | copy-start | bytes 24580
  117.5 3.9 copy-start.37
  117.5 3.9 copy-start.38
  117.5 4.0 copy-start.39
  156.9 5.9 %copy-start.48 = (bf16[16,1,512]{2,0,1:T(8,128)(2,1)S(1)}, bf16[16,1,512]{2,0,1:T(8,128)(2,1)}, u32[]{:S(2)}) copy-start(bf16[16,1,512]{2,0,1:T(8,128)(2,1)} %copy.284) | copy-start | bytes 49156
  156.9 5.9 %copy-start.58 = (s32[2,8]{1,0:T(2,128)S(1)}, s32[2,8]{1,0:T(2,128)}, u32[]{:S(2)}) copy-start(s32[2,8]{1,0:T(2,128)} %reshape.246) | copy-start | bytes 196
  162.9 3.3 copy-start.12
  167.8 3.1 copy-start
  177.0 4.4 copy-start.1
  183.1 3.9 copy-start.13
  187.0 3.3 copy-start.12
  191.9 3.1 copy-start
  196.9 2.4 copy-start.3
  201.2 4.4 copy-start.1
  207.3 3.9 copy-start.13
  217.8 11.1 %copy-start.42 = (bf16[1,4,128,128]{3,2,1,0:T(8,128)(2,1)S(1)}, bf16[1,4,128,128]{3,2,1,0:T(8,128)(2,1)}, u32[]{:S(2)}) copy-start(bf16[1,4,128,128]{3,2,1,0:T(8,128)(2,1)} %get-tuple-element.146) | copy-start | bytes 393220
  217.8 11.1 %copy-start.43 = (bf16[1,4,128,128]{3,2,1,0:T(8,128)(2,1)S(1)}, bf16[1,4,128,128]{3,2,1,0:T(8,128)(2,1)}, u32[]{:S(2)}) copy-start(bf16[1,4,128,128]{3,2,1,0:T(8,128)(2,1)} %get-tuple-element.147) | copy-start | bytes 393220
  217.8 11.1 %copy-start.11 = (bf16[4,128,4,128]{3,2,1,0:T(4,128)(2,1)S(1)}, bf16[4,128,4,128]{3,2,1,0:T(4,128)(2,1)}, u32[]{:S(2)}) copy-start(bf16[4,128,4,128]{3,2,1,0:T(4,128)(2,1)} %copy-done.10) | copy-start | bytes 1572868
  217.8 11.1 %copy-start.35 = (f32[4,4,128,128]{3,2,1,0:T(8,128)S(1)}, f32[4,4,128,128]{3,2,1,0:T(8,128)}, u32[]{:S(2)}) copy-start(f32[4,4,128,128]{3,2,1,0:T(8,128)} %copy-done.34) | copy-start | bytes 3145732
  217.8 226.8 %all-to-all-start.5 = ((bf16[16,2,32768]{2,1,0:T(2,128)(2,1)}), bf16[16,2,32768]{2,1,0:T(2,128)(2,1)}, u32[]{:S(2)}, u32[]{:S(2)}) async-start(bf16[16,2,32768]{2,1,0:T(2,128)(2,1)} %reshape.289), calls=%async_computation.5 | async-start | bytes 4194304 | tf_op jit(solution)/shard_map/all_to_all | solution.py:254
  228.8 114.3 %all-reduce.6.cloned.1.call-start = ((), (), s32[]{:S(2)}) async-start(), calls=%async_computation.6 | async-start | bytes 524288 | tf_op jit(solution)/shard_map/psum | solution.py:31
  228.9 6.9 %copy-start.40 = (bf16[1,1,4,128,128]{4,3,2,1,0:T(8,128)(2,1)S(1)}, bf16[1,1,4,128,128]{4,3,2,1,0:T(8,128)(2,1)}, u32[]{:S(2)}) copy-start(bf16[1,1,4,128,128]{4,3,2,1,0:T(8,128)(2,1)} %get-tuple-element.156) | copy-start | bytes 393220
  228.9 6.9 %copy-start.41 = (bf16[1,1,4,128,128]{4,3,2,1,0:T(8,128)(2,1)S(1)}, bf16[1,1,4,128,128]{4,3,2,1,0:T(8,128)(2,1)}, u32[]{:S(2)}) copy-start(bf16[1,1,4,128,128]{4,3,2,1,0:T(8,128)(2,1)} %get-tuple-element.160) | copy-start | bytes 393220
  229.3 6.5 %copy-start.23 = (f32[4,4,128,128]{3,2,1,0:T(8,128)}, f32[4,4,128,128]{3,2,1,0:T(8,128)S(1)}, u32[]{:S(2)}) copy-start(f32[4,4,128,128]{3,2,1,0:T(8,128)S(1)} %fusion.73) | copy-start | bytes 3145732
  229.3 7.6 %copy-start.22 = (f32[4,4,128,128]{3,2,1,0:T(8,128)S(1)}, f32[4,4,128,128]{3,2,1,0:T(8,128)}, u32[]{:S(2)}) copy-start(f32[4,4,128,128]{3,2,1,0:T(8,128)} %fusion.116) | copy-start | bytes 3145732
  229.4 6.4 %copy-start.24 = (bf16[1,2,4,128,128]{4,3,2,1,0:T(8,128)(2,1)}, bf16[1,2,4,128,128]{4,3,2,1,0:T(8,128)(2,1)S(1)}, u32[]{:S(2)}) copy-start(bf16[1,2,4,128,128]{4,3,2,1,0:T(8,128)(2,1)S(1)} %maximum_bitcast_fusion.3) | copy-start | bytes 786436
  230.2 117.7 %collective-permute-start.2 = (bf16[2,1,4,128,128]{4,3,2,1,0:T(8,128)(2,1)}, bf16[2,1,4,128,128]{4,3,2,1,0:T(8,128)(2,1)}, u32[]{:S(2)}, u32[]{:S(2)}) collective-permute-start(bf16[2,1,4,128,128]{4,3,2,1,0:T(8,128)(2,1)} %get-tuple-element.150), channel_id=1, source_target_pairs={{0,2},{2,4},{4,6},{6,8},{8,10},{10,12},{12,14},{14,16},{16,18},{18... | collective-permute-start | bytes 786440 | tf_op jit(solution)/shard_map/ppermute | solution.py:20
  233.9 114.0 %collective-permute-start.3 = (bf16[2,1,4,128,128]{4,3,2,1,0:T(8,128)(2,1)}, bf16[2,1,4,128,128]{4,3,2,1,0:T(8,128)(2,1)}, u32[]{:S(2)}, u32[]{:S(2)}) collective-permute-start(bf16[2,1,4,128,128]{4,3,2,1,0:T(8,128)(2,1)} %get-tuple-element.151), channel_id=1, source_target_pairs={{2,0},{4,2},{6,4},{8,6},{10,8},{12,10},{14,12},{16,14},{18,16},{20... | collective-permute-start | bytes 786440 | tf_op jit(solution)/shard_map/ppermute | solution.py:22
  236.6 107.6 %copy-start.16 = (bf16[4,128,4,128]{3,2,1,0:T(4,128)(2,1)S(1)}, bf16[4,128,4,128]{3,2,1,0:T(4,128)(2,1)}, u32[]{:S(2)}) copy-start(bf16[4,128,4,128]{3,2,1,0:T(4,128)(2,1)} %reshape.239) | copy-start | bytes 1572868
  236.6 107.6 %copy-start.57 = (f32[4,4,128]{2,1,0:T(4,128)S(1)}, f32[4,4,128]{2,1,0:T(4,128)}, u32[]{:S(2)}) copy-start(f32[4,4,128]{2,1,0:T(4,128)} %copy-done.55) | copy-start | bytes 24580
  236.6 108.7 %copy-start.51 = (f32[4,4,128]{2,1,0:T(4,128)S(1)}, f32[4,4,128]{2,1,0:T(4,128)}, u32[]{:S(2)}) copy-start(f32[4,4,128]{2,1,0:T(4,128)} %copy-done.49) | copy-start | bytes 24580
  236.6 201.9 %all-reduce.8.cloned.1.call-start = ((), (), s32[]{:S(2)}) async-start(), calls=%async_computation.7 | async-start | bytes 1048576 | tf_op jit(solution)/shard_map/psum | solution.py:162
  349.7 90.9 %copy-start.9 = (f32[4,65536]{1,0:T(4,128)S(1)}, f32[4,65536]{1,0:T(4,128)}, u32[]{:S(2)}) copy-start(f32[4,65536]{1,0:T(4,128)} %get-tuple-element.69) | copy-start | bytes 3145732
  352.4 88.2 %copy-start.31 = (f32[1,4,128,128]{3,2,1,0:T(8,128)S(1)}, f32[1,4,128,128]{3,2,1,0:T(8,128)}, u32[]{:S(2)}) copy-start(f32[1,4,128,128]{3,2,1,0:T(8,128)} %get-tuple-element.138) | copy-start | bytes 786436
  (33 other events, 50.7 us)
Sparse Core Ops, SparseCore 0:
  236.7 106.3 all-reduce.5
  348.0 90.4 all-reduce.7
where the time goes:
time: 479 us; the launch traced here: 470 us
  waiting for transfers between devices  221 us (46%)
  local copies, waits for them, and re-layouts  98.1 us (20%)
  starting transfers between devices  57.8 us (12%)
  matrix products  49.5 us (10%)
  other arithmetic  27.9 us (6%)
  between operations  15.2 us (3%)
    psum x1, waiting for transfers between devices, spread_2(): return lax.psum(jnp.where(mine, array, jnp.zeros_like(array)), axis)  105 us
    psum x1, waiting for transfers between devices, shards(): total_key, total_value = lax.psum((part_key, part_value), 'ctx')  86 us
    unnamed x119, local copies, waits for them, and re-layouts  61.9 us
    all_to_all x1, waiting for transfers between devices, shards(): lax.all_to_all(route_rows(grad_blk), 'ctx', split_axis=0, concat_axis=0,...  15 us
    all_to_all x1, starting transfers between devices, shards(): lax.all_to_all(route_rows(query_blk), 'ctx', split_axis=0, concat_axis=0,...  12.4 us
    all_to_all x1, starting transfers between devices, shards(): lax.all_to_all(answers, 'ctx', split_axis=0, concat_axis=0, tiled=True)  11 us
    all_to_all x1, waiting for transfers between devices, shards(): lax.all_to_all(route_rows(query_blk), 'ctx', split_axis=0, concat_axis=0,...  10.6 us
    reshape x8, local copies, waits for them, and re-layouts, heads_major(): array.reshape(slot_count, height, head_count, head_size)  9.61 us
  transfers between devices with their start and end apart: 12, of which 6 were waited for; matrix products, arithmetic and copies ran while one was open for 17% of the time, Pallas kernels for 0%

commit v1 on v0

--- a/solution.py
+++ b/solution.py
@@ -7,6 +7,12 @@
 WINDOW = 2
 GLOBAL = 1
 RANDOM = 3
+
+
+def summed_here(value, axis):
+    parts = lax.all_gather(value, axis, axis=0, tiled=False)
+    result = parts.sum(axis=0)
+    return result
 
 
 def padded(cells, sides, width):
@@ -28,7 +34,7 @@
 
 def spread_2(array, axis, root):
     mine = lax.axis_index(axis) == root
-    return lax.psum(jnp.where(mine, array, jnp.zeros_like(array)), axis)
+    return summed_here(jnp.where(mine, array, jnp.zeros_like(array)), axis)
 
 
 def pair_grads(query_heads, grad_heads, norm_blk, delta_blk, key_heads, value_heads, visible):

time: 479 us -> 434 us (0.906)
  waiting for transfers between devices: 221 us -> 175 us
  starting transfers between devices: 57.8 us -> 65.6 us
  local copies, waits for them, and re-layouts: 98.1 us -> 91.1 us
    psum x1 -> x0, waiting for transfers between devices: 105 us -> none  [spread_2(): return lax.psum(jnp.where(mine, array, jnp.zeros_like(array)), axis)]
    all_to_all x1, waiting for transfers between devices: 10.6 us -> 28.9 us  [shards(): lax.all_to_all(route_rows(query_blk), 'ctx', split_axis=0, concat_axis=0,...]
    all_to_all x1, waiting for transfers between devices: 0.01 us -> 17.5 us  [shards(): lax.all_to_all(answers, 'ctx', split_axis=0, concat_axis=0, tiled=True)]
    psum x1, waiting for transfers between devices: 86 us -> 101 us  [shards(): total_key, total_value = lax.psum((part_key, part_value), 'ctx')]
    all_to_all x1, starting transfers between devices: 11 us -> 18.9 us  [shards(): lax.all_to_all(answers, 'ctx', split_axis=0, concat_axis=0, tiled=True)]
    unnamed x119 -> x89, local copies, waits for them, and re-layouts: 61.9 us -> 60.4 us
  transfers between devices with their start and end apart: 12 -> 12, of which waited for: 6 -> 8; matrix products, arithmetic and copies ran while one was open for 17% -> 35% of each run, Pallas kernels for 0% -> 0%
where the time goes in v1:
time: 434 us; the launch traced here: 425 us
  waiting for transfers between devices  175 us (40%)
  local copies, waits for them, and re-layouts  91.1 us (21%)
  starting transfers between devices  65.6 us (15%)
  matrix products  48.6 us (11%)
  other arithmetic  29 us (7%)
  between operations  15 us (3%)
    psum x1, waiting for transfers between devices, shards(): total_key, total_value = lax.psum((part_key, part_value), 'ctx')  101 us
    unnamed x89, local copies, waits for them, and re-layouts  60.4 us
    all_to_all x1, waiting for transfers between devices, shards(): lax.all_to_all(route_rows(query_blk), 'ctx', split_axis=0, concat_axis=0,...  28.9 us
    all_to_all x1, starting transfers between devices, shards(): lax.all_to_all(answers, 'ctx', split_axis=0, concat_axis=0, tiled=True)  18.9 us
    all_to_all x1, waiting for transfers between devices, shards(): lax.all_to_all(answers, 'ctx', split_axis=0, concat_axis=0, tiled=True)  17.5 us
    all_to_all x1, waiting for transfers between devices, shards(): lax.all_to_all(route_rows(grad_blk), 'ctx', split_axis=0, concat_axis=0,...  17.3 us
    all_to_all x1, starting transfers between devices, shards(): lax.all_to_all(route_rows(query_blk), 'ctx', split_axis=0, concat_axis=0,...  11.7 us
    dot_general x2, matrix products, owner_step(): jnp.einsum('gs,gx->sx', choose_float, term_key.reshape(group_size, -1), p...  8.85 us
  transfers between devices with their start and end apart: 12, of which 8 were waited for; matrix products, arithmetic and copies ran while one was open for 35% of the time, Pallas kernels for 0%

profile of v1, /device:TPU:1, one launch (start us, length us, event | category | flops | bytes accessed | tf_op | source)
XLA Modules:
  0.0 425.1 jit_solution(12646689609900593393)
XLA Ops:
  8.8 7.3 %all-to-all-start = ((s32[16,1,1]{2,1,0:T(1,128)}), s32[16,1,1]{2,1,0:T(1,128)S(1)}, u32[]{:S(2)}, u32[]{:S(2)}) async-start(s32[16,1,1]{2,1,0:T(1,128)} %copy.127), calls=%async_computation | async-start | bytes 16384 | tf_op jit(solution)/shard_map/all_to_all | solution.py:198
  21.9 5.6 %all-to-all-start.4 = ((bf16[16,2,256]{2,1,0:T(2,128)(2,1)}), bf16[16,2,256]{2,1,0:T(2,128)(2,1)S(1)}, u32[]{:S(2)}, u32[]{:S(2)}) async-start(bf16[16,2,256]{2,1,0:T(2,128)(2,1)} %reshape.296), calls=%async_computation.4 | async-start | bytes 32768 | tf_op jit(solution)/shard_map/all_to_all | solution.py:197
  29.1 4.3 %all-to-all-done.4 = bf16[16,2,256]{2,1,0:T(2,128)(2,1)S(1)} async-done(((bf16[16,2,256]{2,1,0:T(2,128)(2,1)}), bf16[16,2,256]{2,1,0:T(2,128)(2,1)S(1)}, u32[]{:S(2)}, u32[]{:S(2)}) %all-to-all-start.4) | async-done | bytes 16416 | tf_op jit(solution)/shard_map/all_to_all | solution.py:197
  33.3 4.0 all-to-all-start.2
  38.2 2.9 reduce.9
  41.1 4.0 reshape.294
  45.1 6.2 %all-to-all-start.3 = ((bf16[16,2,32768]{2,1,0:T(2,128)(2,1)}), bf16[16,2,32768]{2,1,0:T(2,128)(2,1)S(1)}, u32[]{:S(2)}, u32[]{:S(2)}) async-start(bf16[16,2,32768]{2,1,0:T(2,128)(2,1)} %reshape.294), calls=%async_computation.3 | async-start | bytes 4194304 | tf_op jit(solution)/shard_map/all_to_all | solution.py:195
  52.2 2.0 reshape.252
  56.2 2.0 collective-permute-start.1
  58.2 3.6 collective-permute-start
  61.8 2.0 reshape.248
  64.9 2.2 fusion.24
  67.1 4.5 %reduce.7 = bf16[16,65536]{1,0:T(8,128)(2,1)} reduce(bf16[16,1,65536]{2,0,1:T(8,128)(2,1)} %fusion.24, bf16[]{:T(256)} %broadcast.231), dimensions={1}, to_apply=%copy.128.reduce_sub_computation | reduce | bytes 4194306 | tf_op jit(solution)/shard_map/all_to_all | solution.py:194
  71.6 4.0 reshape.290
  75.5 17.3 %all-to-all-done.3 = bf16[16,2,32768]{2,1,0:T(2,128)(2,1)S(1)} async-done(((bf16[16,2,32768]{2,1,0:T(2,128)(2,1)}), bf16[16,2,32768]{2,1,0:T(2,128)(2,1)S(1)}, u32[]{:S(2)}, u32[]{:S(2)}) %all-to-all-start.3) | async-done | bytes 2097184 | tf_op jit(solution)/shard_map/all_to_all | solution.py:195
  92.8 11.7 %all-to-all-start.1 = ((bf16[16,2,32768]{2,1,0:T(2,128)(2,1)}), bf16[16,2,32768]{2,1,0:T(2,128)(2,1)}, u32[]{:S(2)}, u32[]{:S(2)}) async-start(bf16[16,2,32768]{2,1,0:T(2,128)(2,1)} %reshape.290), calls=%async_computation.1 | async-start | bytes 4194304 | tf_op jit(solution)/shard_map/all_to_all | solution.py:194
  105.0 1.8 copy_bitcast_fusion.6
  111.8 1.7 slice_bitcast_fusion.6
  114.2 6.8 %reshape.295 = bf16[16,1,65536]{2,1,0:T(2,128)(2,1)} reshape(bf16[16,2,32768]{2,1,0:T(2,128)(2,1)S(1)} %all-to-all-done.3) | data formatting | bytes 4194304
  121.1 4.6 %copy.278 = bf16[16,1,65536]{2,0,1:T(8,128)(2,1)S(1)} copy(bf16[16,1,65536]{2,1,0:T(2,128)(2,1)} %reshape.295) | data formatting | bytes 4194304
  125.7 28.9 %all-to-all-done.1 = bf16[16,2,32768]{2,1,0:T(2,128)(2,1)} async-done(((bf16[16,2,32768]{2,1,0:T(2,128)(2,1)}), bf16[16,2,32768]{2,1,0:T(2,128)(2,1)}, u32[]{:S(2)}, u32[]{:S(2)}) %all-to-all-start.1) | async-done | bytes 2097184 | tf_op jit(solution)/shard_map/all_to_all | solution.py:194
  154.5 10.6 %reshape.291 = bf16[16,1,65536]{2,1,0:T(2,128)(2,1)} reshape(bf16[16,2,32768]{2,1,0:T(2,128)(2,1)} %all-to-all-done.1) | data formatting | bytes 4194304
  165.1 5.8 %copy.279 = bf16[16,1,65536]{2,0,1:T(8,128)(2,1)} copy(bf16[16,1,65536]{2,1,0:T(2,128)(2,1)} %reshape.291) | data formatting | bytes 4194304
  170.9 50.5 %while.15 = (s32[]{:T(128)}, f32[4,65536]{1,0:T(4,128)}, f32[4,65536]{1,0:T(4,128)}, bf16[2,8,65536]{2,1,0:T(8,128)(2,1)}, s32[2,8]{1,0:T(2,128)}, /*index=5*/bf...) while((s32[]{:T(128)}, f32[4,65536]{1,0:T(4,128)}, ...), condition=%wide.region_5.6_spmd.clone, body=%wide.region_4.5_spmd.clone.sunk | while | flops 737157248 | bytes 105006344 | solution.py:248
  171.7 1.6 convolution_convert_fusion.8
  177.1 1.9 convolution_convert_fusion.9
  182.1 2.3 constant_dynamic-update-slice_fusion.2
  184.4 1.8 convolution_multiply_fusion.8
  186.3 4.4 %convolution_add_fusion.7 = f32[4,65536]{1,0:T(4,128)S(1)} fusion(f32[1,8,512,128]{3,2,1,0:T(8,128)} %bitcast.274, f32[4,65536]{1,0:T(4,128)S(1)} %copy-done.4, pred[]{:T(512)S(6)} %compare.11, s32[4]{0:T(128)S(1)} %iota_add_fusion.2, s32[8]{0:T(128)S(1)} %get-tuple-element.256), kind=kOutput, calls=%fused_computation.4.clone.1 | convolution fusion | flops 25690144 | bytes 4194353 | tf_op jit(solution)/shard_map/while/body/eval_jaxpr/gs,gx->sx/dot_general | solution.py:230
  192.3 2.9 convolution_add_fusion.8
  202.2 1.9 convolution_convert_fusion.9
  207.2 2.4 constant_dynamic-update-slice_fusion.2
  209.6 1.8 convolution_multiply_fusion.8
  211.5 4.4 %convolution_add_fusion.7 = f32[4,65536]{1,0:T(4,128)S(1)} fusion(f32[1,8,512,128]{3,2,1,0:T(8,128)} %bitcast.274, f32[4,65536]{1,0:T(4,128)S(1)} %copy-done.4, pred[]{:T(512)S(6)} %compare.11, s32[4]{0:T(128)S(1)} %iota_add_fusion.2, s32[8]{0:T(128)S(1)} %get-tuple-element.256), kind=kOutput, calls=%fused_computation.4.clone.1 | convolution fusion | flops 25690144 | bytes 4194353 | tf_op jit(solution)/shard_map/while/body/eval_jaxpr/gs,gx->sx/dot_general | solution.py:230
  217.5 2.9 convolution_add_fusion.8
  221.4 3.8 reduce.11
  225.3 2.8 reshape.298
  228.0 18.9 %all-to-all-start.5 = ((bf16[16,2,32768]{2,1,0:T(2,128)(2,1)}), bf16[16,2,32768]{2,1,0:T(2,128)(2,1)S(1)}, u32[]{:S(2)}, u32[]{:S(2)}) async-start(bf16[16,2,32768]{2,1,0:T(2,128)(2,1)} %reshape.298), calls=%async_computation.5 | async-start | bytes 4194304 | tf_op jit(solution)/shard_map/all_to_all | solution.py:260
  247.3 1.8 fusion.46
  253.0 3.5 collective-permute-start.2
  256.5 1.9 collective-permute-start.3
  259.8 2.9 collective-permute-done.2
  262.6 3.6 collective-permute-done.3
  270.9 17.5 %all-to-all-done.5 = bf16[16,2,32768]{2,1,0:T(2,128)(2,1)S(1)} async-done(((bf16[16,2,32768]{2,1,0:T(2,128)(2,1)}), bf16[16,2,32768]{2,1,0:T(2,128)(2,1)S(1)}, u32[]{:S(2)}, u32[]{:S(2)}) %all-to-all-start.5) | async-done | bytes 2097184 | tf_op jit(solution)/shard_map/all_to_all | solution.py:260
  288.4 6.8 %reshape.299 = bf16[16,1,65536]{2,1,0:T(2,128)(2,1)} reshape(bf16[16,2,32768]{2,1,0:T(2,128)(2,1)S(1)} %all-to-all-done.5) | data formatting | bytes 4194304
  295.2 4.5 %copy.277 = bf16[16,1,65536]{2,0,1:T(8,128)(2,1)S(1)} copy(bf16[16,1,65536]{2,1,0:T(2,128)(2,1)} %reshape.299) | data formatting | bytes 4194304
  301.7 3.0 reduce_sum.52
  311.4 100.6 %all-reduce.5.cloned.1.call-done = (f32[1,4,128,128]{3,2,1,0:T(8,128)}, f32[1,4,128,128]{3,2,1,0:T(8,128)}) async-done(((f32[1,4,128,128]{3,2,1,0:T(8,128)}, f32[1,4,128,128]{3,2,1,0:T(8,128)}), (f32[1,4,128,128]{3,2,1,0:T(8,128)}, f32[1,4,128,128]{3,2,1,0:T(8,128)})) %all-reduce.5.cloned.1.call-update) | async-done | bytes 524304 | tf_op jit(solution)/shard_map/psum | solution.py:168
  (222 shorter events, 65.9 us)
Async XLA Ops:
  8.8 13.0 %all-to-all-start = ((s32[16,1,1]{2,1,0:T(1,128)}), s32[16,1,1]{2,1,0:T(1,128)S(1)}, u32[]{:S(2)}, u32[]{:S(2)}) async-start(s32[16,1,1]{2,1,0:T(1,128)} %copy.127), calls=%async_computation | async-start | bytes 16384 | tf_op jit(solution)/shard_map/all_to_all | solution.py:198
  16.3 11.3 %copy-start.38 = (bf16[4,512]{1,0:T(4,128)(2,1)S(1)}, bf16[4,512]{1,0:T(4,128)(2,1)}, u32[]{:S(2)}) copy-start(bf16[4,512]{1,0:T(4,128)(2,1)} %param.14) | copy-start | bytes 12292
  17.4 10.4 %copy-start.10 = (bf16[4,128,4,128]{3,2,1,0:T(4,128)(2,1)}, bf16[4,128,4,128]{3,2,1,0:T(4,128)(2,1)S(1)}, u32[]{:S(2)}) copy-start(bf16[4,128,4,128]{3,2,1,0:T(4,128)(2,1)S(1)} %reshape.251) | copy-start | bytes 1572868
  19.1 45.8 %copy-start.36 = (pred[16,4]{0,1:T(4,128)(4,1)}, pred[16,4]{0,1:T(4,128)(4,1)S(1)}, u32[]{:S(2)}) copy-start(pred[16,4]{0,1:T(4,128)(4,1)S(1)} %fusion.98) | copy-start | bytes 196
  21.9 11.5 %all-to-all-start.4 = ((bf16[16,2,256]{2,1,0:T(2,128)(2,1)}), bf16[16,2,256]{2,1,0:T(2,128)(2,1)S(1)}, u32[]{:S(2)}, u32[]{:S(2)}) async-start(bf16[16,2,256]{2,1,0:T(2,128)(2,1)} %reshape.296), calls=%async_computation.4 | async-start | bytes 32768 | tf_op jit(solution)/shard_map/all_to_all | solution.py:197
  33.3 11.7 %all-to-all-start.2 = ((bf16[16,2,256]{2,1,0:T(2,128)(2,1)}), bf16[16,2,256]{2,1,0:T(2,128)(2,1)S(1)}, u32[]{:S(2)}, u32[]{:S(2)}) async-start(bf16[16,2,256]{2,1,0:T(2,128)(2,1)} %reshape.292), calls=%async_computation.2 | async-start | bytes 32768 | tf_op jit(solution)/shard_map/all_to_all | solution.py:196
  45.1 6.2 %copy-start.27 = (bf16[512,512]{1,0:T(8,128)(2,1)S(1)}, bf16[512,512]{1,0:T(8,128)(2,1)}, u32[]{:S(2)}) copy-start(bf16[512,512]{1,0:T(8,128)(2,1)} %param.10) | copy-start | bytes 1572868
  45.1 47.7 %all-to-all-start.3 = ((bf16[16,2,32768]{2,1,0:T(2,128)(2,1)}), bf16[16,2,32768]{2,1,0:T(2,128)(2,1)S(1)}, u32[]{:S(2)}, u32[]{:S(2)}) async-start(bf16[16,2,32768]{2,1,0:T(2,128)(2,1)} %reshape.294), calls=%async_computation.3 | async-start | bytes 4194304 | tf_op jit(solution)/shard_map/all_to_all | solution.py:195
  56.2 54.6 %collective-permute-start.1 = (bf16[2,1,4,128,128]{4,3,2,1,0:T(8,128)(2,1)S(1)}, bf16[2,1,4,128,128]{4,3,2,1,0:T(8,128)(2,1)}, u32[]{:S(2)}, u32[]{:S(2)}) collective-permute-start(bf16[2,1,4,128,128]{4,3,2,1,0:T(8,128)(2,1)S(1)} %get-tuple-element.165), channel_id=1, source_target_pairs={{2,0},{4,2},{6,4},{8,6},{10,8},{12,10},{14,12},{16,14},{18,16},{20... | collective-permute-start | bytes 786440 | tf_op jit(solution)/shard_map/ppermute | solution.py:28
  58.2 191.8 %collective-permute-start = (bf16[2,1,4,128,128]{4,3,2,1,0:T(8,128)(2,1)}, bf16[2,1,4,128,128]{4,3,2,1,0:T(8,128)(2,1)}, u32[]{:S(2)}, u32[]{:S(2)}) collective-permute-start(bf16[2,1,4,128,128]{4,3,2,1,0:T(8,128)(2,1)} %get-tuple-element.164), channel_id=1, source_target_pairs={{0,2},{2,4},{4,6},{6,8},{8,10},{10,12},{12,14},{14,16},{16,18},{18... | collective-permute-start | bytes 786440 | tf_op jit(solution)/shard_map/ppermute | solution.py:26
  92.8 61.7 %all-to-all-start.1 = ((bf16[16,2,32768]{2,1,0:T(2,128)(2,1)}), bf16[16,2,32768]{2,1,0:T(2,128)(2,1)}, u32[]{:S(2)}, u32[]{:S(2)}) async-start(bf16[16,2,32768]{2,1,0:T(2,128)(2,1)} %reshape.290), calls=%async_computation.1 | async-start | bytes 4194304 | tf_op jit(solution)/shard_map/all_to_all | solution.py:194
  104.5 197.2 %all-gather.2.cloned.1.call-start = ((), (), s32[]{:S(2)}) async-start(), calls=%async_computation.6 | async-start | bytes 4456448 | tf_op jit(solution)/shard_map/all_gather | solution.py:13
  171.1 3.7 copy-start.12
  174.9 2.2 copy-start.2
  177.1 3.2 copy-start
  182.1 2.3 copy-start.3
  184.4 1.8 copy-start.4
  186.3 4.4 %copy-start.1 = (f32[8,4,128,128]{3,2,1,0:T(8,128)S(1)}, f32[8,4,128,128]{3,2,1,0:T(8,128)}, u32[]{:S(2)}) copy-start(f32[8,4,128,128]{3,2,1,0:T(8,128)} %copy-done) | copy-start | bytes 6291460 | tf_op jit(solution)/shard_map/while
  192.3 3.9 copy-start.13
  196.2 3.6 copy-start.12
  200.0 2.2 copy-start.2
  202.2 3.1 copy-start
  207.2 2.4 copy-start.3
  209.6 1.8 copy-start.4
  211.5 4.4 %copy-start.1 = (f32[8,4,128,128]{3,2,1,0:T(8,128)S(1)}, f32[8,4,128,128]{3,2,1,0:T(8,128)}, u32[]{:S(2)}) copy-start(f32[8,4,128,128]{3,2,1,0:T(8,128)} %copy-done) | copy-start | bytes 6291460 | tf_op jit(solution)/shard_map/while
  217.5 3.9 copy-start.13
  228.0 19.2 %copy-start.39 = (bf16[4,512]{1,0:T(4,128)(2,1)S(1)}, bf16[4,512]{1,0:T(4,128)(2,1)}, u32[]{:S(2)}) copy-start(bf16[4,512]{1,0:T(4,128)(2,1)} %param.14) | copy-start | bytes 12292
  228.0 60.4 %all-to-all-start.5 = ((bf16[16,2,32768]{2,1,0:T(2,128)(2,1)}), bf16[16,2,32768]{2,1,0:T(2,128)(2,1)S(1)}, u32[]{:S(2)}, u32[]{:S(2)}) async-start(bf16[16,2,32768]{2,1,0:T(2,128)(2,1)} %reshape.298), calls=%async_computation.5 | async-start | bytes 4194304 | tf_op jit(solution)/shard_map/all_to_all | solution.py:260
  246.9 2.1 copy-start.11
  246.9 2.1 copy-start.14
  246.9 165.0 %all-reduce.5.cloned.1.call-start = ((), (), s32[]{:S(2)}) async-start(), calls=%async_computation.7 | async-start | bytes 1048576 | tf_op jit(solution)/shard_map/psum | solution.py:168
  247.2 3.8 copy-start.40
  247.2 2.4 copy-start.18
  249.1 2.0 copy-start.15
  249.1 2.0 copy-start.43
  249.6 2.0 copy-start.24
  253.0 9.6 %collective-permute-start.2 = (bf16[2,1,4,128,128]{4,3,2,1,0:T(8,128)(2,1)S(1)}, bf16[2,1,4,128,128]{4,3,2,1,0:T(8,128)(2,1)S(1)}, u32[]{:S(2)}, u32[]{:S(2)}) collective-permute-start(bf16[2,1,4,128,128]{4,3,2,1,0:T(8,128)(2,1)S(1)} %get-tuple-element.150), channel_id=1, source_target_pairs={{0,2},{2,4},{4,6},{6,8},{8,10},{10,12},{12,14},{14,16},{16,18},{18... | collective-permute-start | bytes 786440 | tf_op jit(solution)/shard_map/ppermute | solution.py:26
  256.5 9.7 %collective-permute-start.3 = (bf16[2,1,4,128,128]{4,3,2,1,0:T(8,128)(2,1)S(1)}, bf16[2,1,4,128,128]{4,3,2,1,0:T(8,128)(2,1)S(1)}, u32[]{:S(2)}, u32[]{:S(2)}) collective-permute-start(bf16[2,1,4,128,128]{4,3,2,1,0:T(8,128)(2,1)S(1)} %get-tuple-element.151), channel_id=1, source_target_pairs={{2,0},{4,2},{6,4},{8,6},{10,8},{12,10},{14,12},{16,14},{18,16},{20... | collective-permute-start | bytes 786440 | tf_op jit(solution)/shard_map/ppermute | solution.py:28
  268.2 1.7 copy-start.6
  301.7 3.1 copy-start.16
  301.7 3.1 copy-start.41
  301.7 3.1 copy-start.42
  306.3 2.3 copy-start.19
  310.1 102.9 %copy-start.21 = (f32[4,4,128,128]{3,2,1,0:T(8,128)S(1)}, f32[4,4,128,128]{3,2,1,0:T(8,128)}, u32[]{:S(2)}) copy-start(f32[4,4,128,128]{3,2,1,0:T(8,128)} %copy-done.20) | copy-start | bytes 3145732
  310.1 102.9 %copy-start.22 = (f32[1,4,512,128]{3,2,1,0:T(8,128)S(1)}, f32[1,4,512,128]{3,2,1,0:T(8,128)}, u32[]{:S(2)}) copy-start(f32[1,4,512,128]{3,2,1,0:T(8,128)} %copy.166) | copy-start | bytes 3145732
  412.9 2.9 copy-start.31
  414.5 1.7 copy-start.30
  414.5 1.8 copy-start.32
  (18 other events, 22.7 us)
Sparse Core Ops, SparseCore 0:
  114.4 67.5 all-gather.1
  308.7 103.1 all-reduce.4
